TPU v7x, 512 devices: a whole 4x4x16 slice. The times are simulated.
512 devices in a mesh: smp: 16 (over z), par: 32 (over x, y, core).
Axes of the slice: x: 4, y: 4, z: 16, core: 2. Of those that a mesh axis runs over, the one named last changes fastest.
Arguments:
- jacobian: bfloat16 [4096, 16384], P('smp', 'par'), may hold values from -52 to 52
Outputs:
- panel_factor: float32 [4096, 512], P('smp')
- schur_part: float32 [4096, 4096], P('smp', 'par')
All inputs are finite; a program needn't handle non-finite values.
Results may differ from a plain program's by a relative error of at most 0.0022.
Values may be sent and summed in bfloat16 or wider, within the bound.
No kernel may reach another device: no remote copies, remote signals or barrier semaphores. Data moves between devices by JAX's collectives and lax.ppermute only.
A program may use at most 64 MiB of HBM per device.

v0:
```python
import jax
import jax.numpy as jnp
from jax import lax
from jax.sharding import PartitionSpec as P

PANEL = 512
shift_scale = 0.01


def shards(jacobian):
    row_count, par_width = jacobian.shape
    par_count = lax.axis_size("par")
    smp_count = lax.axis_size("smp")
    sample_total = row_count * smp_count
    param_total = par_width * par_count
    col_width = sample_total // par_count
    row_index = lax.axis_index("smp")
    col_index = lax.axis_index("par")
    widened = jacobian.astype(jnp.float32)
    col_mean = lax.psum(jnp.sum(widened, axis=0), "smp") / sample_total
    centered = (widened - col_mean).astype(jnp.bfloat16)
    gathered = lax.all_gather(centered, "smp", axis=0, tiled=True)
    gram_tile = lax.psum_scatter(
        lax.dot_general(
            gathered, centered, (((1,), (1,)), ((), ())), preferred_element_type=jnp.float32
        )
        / param_total,
        "par",
        scatter_dimension=0,
        tiled=True,
    ).T
    global_rows = row_index * row_count + jnp.arange(row_count, dtype=jnp.int32)
    global_cols = col_index * col_width + jnp.arange(col_width, dtype=jnp.int32)
    diag_mask = global_rows[:, None] == global_cols[None, :]
    trace_total = lax.psum(jnp.sum(jnp.where(diag_mask, gram_tile, 0.0)), ("smp", "par"))
    shift_value = shift_scale * trace_total / sample_total
    shifted = gram_tile + jnp.where(diag_mask, shift_value, 0.0)
    col_keep = (col_index < PANEL // col_width).astype(jnp.float32)
    start_col = jnp.minimum(col_index, PANEL // col_width - 1) * col_width
    placed_rows = lax.dynamic_update_slice(
        jnp.zeros((row_count, PANEL), jnp.float32), shifted * col_keep, (jnp.int32(0), start_col)
    )
    panel_rows = lax.psum(placed_rows, "par")
    row_keep = (row_index < PANEL // row_count).astype(jnp.float32)
    start_row = jnp.minimum(row_index, PANEL // row_count - 1) * row_count
    top_square = lax.dynamic_update_slice(
        jnp.zeros((PANEL, PANEL), jnp.float32), panel_rows * row_keep, (start_row, jnp.int32(0))
    )
    top_band = lax.dynamic_update_slice(
        jnp.zeros((PANEL, col_width), jnp.float32), shifted * row_keep, (start_row, jnp.int32(0))
    )
    square, band_rows = lax.psum((top_square, top_band), "smp")
    factor = jnp.linalg.cholesky(square)
    panel_out = jax.scipy.linalg.solve_triangular(factor, panel_rows.T, lower=True).T
    band_factor = jax.scipy.linalg.solve_triangular(factor, band_rows, lower=True)
    schur_tile = shifted - jnp.dot(panel_out, band_factor, precision=lax.Precision.HIGHEST)
    return (panel_out, schur_tile)


def solution(mesh):
    placed = (P("smp", "par"),)
    return jax.shard_map(
        shards,
        mesh=mesh,
        in_specs=placed,
        out_specs=(P("smp", None), P("smp", "par")),
        check_vma=False,
    )
```

profile of v0, /device:TPU:2, one launch (start us, length us, event | category | flops | bytes accessed | tf_op | source)
XLA Modules:
  0.0 757.3 jit_solution(15600301314958486580)
XLA Ops:
  7.2 1.0 convert_reduce_fusion
  8.2 36.5 %psum.35 = f32[512]{0:T(512)S(1)} all-reduce(f32[512]{0:T(512)S(1)} %convert_reduce_fusion), channel_id=1, replica_groups=mesh['smp'=16,'par'=32] {'smp'}, use_global_device_ids=true, to_apply=%region_1.0 | all-reduce | flops 512 | bytes 4096 | tf_op jit(solution)/shard_map/psum | solution.py:20
  44.7 1.7 fusion.1
  46.5 74.9 %all-gather.2.cloned.1.call-done = bf16[4096,512]{1,0:T(8,128)(2,1)} async-done(((bf16[256,512]{1,0:T(8,128)(2,1)}), bf16[4096,512]{1,0:T(8,128)(2,1)}) %all-gather.2.cloned.1.call-update) | async-done | bytes 4194320 | tf_op jit(solution)/shard_map/all_gather | solution.py:22
  121.4 5.4 convolution_multiply_fusion
  126.9 101.3 %reduce-scatter.2.cloned.1.call-done = f32[128,256]{1,0:T(8,128)} async-done(((f32[4096,256]{1,0:T(8,128)}), f32[128,256]{1,0:T(8,128)}) %reduce-scatter.2.cloned.1.call-update) | async-done | bytes 131088 | tf_op jit(solution)/shard_map/reduce_scatter | solution.py:23
  228.2 1.6 fusion.29
  229.8 101.8 %psum.36 = f32[]{:T(128)} all-reduce(f32[]{:T(128)} %fusion.29), channel_id=1, replica_groups=mesh['smp'=16,'par'=32] {'smp','par'}, use_global_device_ids=true, to_apply=%region_4.5 | all-reduce | flops 1 | bytes 8 | tf_op jit(solution)/shard_map/psum | solution.py:35
  332.3 1.0 multiply_dynamic-update-slice_fusion.1
  333.4 0.8 copy-done.2
  334.4 130.4 %all-reduce.5.cloned.1.call-done = f32[256,512]{0,1:T(8,128)} async-done(((f32[256,512]{0,1:T(8,128)}), f32[256,512]{0,1:T(8,128)}) %all-reduce.5.cloned.1.call-update) | async-done | bytes 524304 | tf_op jit(solution)/shard_map/psum | solution.py:43
  464.9 1.1 multiply_dynamic-update-slice_fusion
  466.0 1.0 copy-done
  467.1 140.6 %all-reduce.7.cloned.1.call-done = (f32[512,512]{0,1:T(8,128)}, f32[512,128]{0,1:T(8,128)}) async-done(((f32[512,512]{0,1:T(8,128)}, f32[512,128]{0,1:T(8,128)}), (f32[512,512]{0,1:T(8,128)}, f32[512,128]{0,1:T(8,128)})) %all-reduce.7.cloned.1.call-update) | async-done | bytes 1310736 | tf_op jit(solution)/shard_map/psum | solution.py:52
  607.7 1.6 copy.3
  609.3 1.4 fusion
  610.7 11.7 %cholesky.103 = f32[128,128]{1,0:T(8,128)S(1)} custom-call(f32[128,128]{1,0:T(8,128)S(1)} %cholesky.263), custom_call_target="Cholesky" | custom-call | tf_op jit(solution)/shard_map/jit(cholesky)/cholesky | solution.py:53
  622.5 9.8 %custom-call.34 = f32[1,128,128]{1,2,0:T(8,128)S(1)} custom-call(f32[1,128,128]{2,1,0:T(8,128)S(1)} %get-tuple-element.35), custom_call_target="InvertDiagBlocksLowerTriangular" | custom-call | tf_op jit(solution)/shard_map/jit(cholesky)/cholesky | solution.py:53
  633.0 11.7 %cholesky.215 = f32[128,128]{1,0:T(8,128)S(1)} custom-call(f32[128,128]{1,0:T(8,128)S(1)} %cholesky.267), custom_call_target="Cholesky" | custom-call | tf_op jit(solution)/shard_map/jit(cholesky)/cholesky | solution.py:53
  645.2 10.0 %custom-call.35 = f32[1,128,128]{1,2,0:T(8,128)S(1)} custom-call(f32[1,128,128]{2,1,0:T(8,128)S(1)} %get-tuple-element.33), custom_call_target="InvertDiagBlocksLowerTriangular" | custom-call | tf_op jit(solution)/shard_map/jit(cholesky)/cholesky | solution.py:53
  656.2 11.7 %cholesky.236 = f32[128,128]{1,0:T(8,128)S(1)} custom-call(f32[128,128]{1,0:T(8,128)S(1)} %cholesky.272), custom_call_target="Cholesky" | custom-call | tf_op jit(solution)/shard_map/jit(cholesky)/cholesky | solution.py:53
  668.0 9.8 %custom-call.36 = f32[1,128,128]{1,2,0:T(8,128)S(1)} custom-call(f32[1,128,128]{2,1,0:T(8,128)S(1)} %get-tuple-element.31), custom_call_target="InvertDiagBlocksLowerTriangular" | custom-call | tf_op jit(solution)/shard_map/jit(cholesky)/cholesky | solution.py:53
  678.6 11.9 %cholesky.253 = f32[128,128]{1,0:T(8,128)S(1)} custom-call(f32[128,128]{1,0:T(8,128)S(1)} %convolution_subtract_fusion.9), custom_call_target="Cholesky" | custom-call | tf_op jit(solution)/shard_map/jit(cholesky)/cholesky | solution.py:53
  690.7 0.7 compare_reduce_fusion.1
  695.4 8.8 %while.1 = (s32[]{:T(128)}, f32[512,512]{0,1:T(8,128)S(1)}, s32[4,2]{0,1:T(2,128)S(1)}, f32[4,128,128]{2,1,0:T(8,128)S(1)}, s32[]{:T(128)}) while((s32[]{:T(128)}, f32[512,512]{0,1:T(8,128)S(1)}, s32[4,2]{0,1:T(2,128)S(1)}, f32[4,128,128]{2,1,0:T(8,128)S(1)}, s32[]{:T(128)}) %tuple.30), condition=%wide.while_cond, body=%wide.while_body.sunk | while | flops 2 | bytes 393321 | solution.py:54
  696.1 1.4 dynamic-slice.7
  698.3 1.4 dynamic-slice.7
  700.5 1.4 dynamic-slice.7
  702.6 1.4 dynamic-slice.7
  704.2 39.3 %custom-call.37 = f32[4,128,128]{1,2,0:T(8,128)S(1)} custom-call(f32[4,128,128]{2,1,0:T(8,128)S(1)} %get-tuple-element.9), custom_call_target="InvertDiagBlocksLowerTriangular" | custom-call | tf_op jit(solution)/shard_map/jit(_solve_triangular)/triangular_solve | solution.py:54
  749.0 0.8 copy.14
  749.8 1.0 copy.13
  (85 shorter events, 13.6 us)
Async XLA Ops:
  7.2 114.2 %all-gather.2.cloned.1.call-start = ((), (), s32[]{:S(2)}) async-start(), calls=%async_computation.1 | async-start | bytes 4456448 | tf_op jit(solution)/shard_map/all_gather | solution.py:22
  46.5 181.7 %reduce-scatter.2.cloned.1.call-start = ((), (), s32[]{:S(2)}) async-start(), calls=%async_computation.2 | async-start | bytes 4325376 | tf_op jit(solution)/shard_map/reduce_scatter | solution.py:23
  126.8 337.9 %all-reduce.5.cloned.1.call-start = ((), (), s32[]{:S(2)}) async-start(), calls=%async_computation.3 | async-start | bytes 1048576 | tf_op jit(solution)/shard_map/psum | solution.py:43
  333.3 0.8 copy-start.2
  333.4 132.6 %copy-start.3 = (f32[512,128]{0,1:T(8,128)}, f32[512,128]{0,1:T(8,128)S(1)}, u32[]{:S(2)}) copy-start(f32[512,128]{0,1:T(8,128)S(1)} %get-tuple-element.28) | copy-start | bytes 786436
  334.2 273.6 %all-reduce.7.cloned.1.call-start = ((), (), s32[]{:S(2)}) async-start(), calls=%async_computation.4 | async-start | bytes 2621440 | tf_op jit(solution)/shard_map/psum | solution.py:52
  466.0 1.0 copy-start
  645.0 98.5 %copy-start.5 = (f32[512,128]{0,1:T(8,128)S(1)}, f32[512,128]{0,1:T(8,128)}, u32[]{:S(2)}) copy-start(f32[512,128]{0,1:T(8,128)} %get-tuple-element.25) | copy-start | bytes 786436
  655.6 90.3 %copy-start.1 = (f32[256,512]{0,1:T(8,128)S(1)}, f32[256,512]{0,1:T(8,128)}, u32[]{:S(2)}) copy-start(f32[256,512]{0,1:T(8,128)} %all-reduce.5.cloned.1.call-done) | copy-start | bytes 1572868
  695.4 53.0 %copy-start.4 = (f32[128,256]{1,0:T(8,128)S(1)}, f32[128,256]{1,0:T(8,128)}, u32[]{:S(2)}) copy-start(f32[128,256]{1,0:T(8,128)} %reduce-scatter.2.cloned.1.call-done) | copy-start | bytes 393220
Sparse Core Ops, SparseCore 0:
  46.6 74.7 all-gather.1
  126.9 101.1 reduce-scatter.1
  334.3 130.4 all-reduce.4
  467.2 140.4 all-reduce.6
where the time goes:
time: 758 us; the launch traced here: 757 us
  waiting for transfers between devices  447 us (59%)
  blocking collectives  138 us (18%)
  other arithmetic  126 us (17%)
  between operations  17.4 us (2%)
  local copies, waits for them, and re-layouts  14.6 us (2%)
  matrix products  13.1 us (2%)
    psum x1, waiting for transfers between devices, shards(): square, band_rows = lax.psum((top_square, top_band), 'smp')  141 us
    psum x1, waiting for transfers between devices, shards(): panel_rows = lax.psum(placed_rows, 'par')  130 us
    psum x1, blocking collectives, shards(): lax.psum(jnp.sum(jnp.where(diag_mask, gram_tile, 0.0)), ('smp', 'par'))  102 us
    reduce_scatter x1, waiting for transfers between devices, shards(): lax.psum_scatter(lax.dot_general(gathered, centered, (((1,), (1,)), ((),...  101 us
    another operation x14, other arithmetic, shards(): factor = jnp.linalg.cholesky(square)  78.8 us
    all_gather x1, waiting for transfers between devices, shards(): gathered = lax.all_gather(centered, 'smp', axis=0, tiled=True)  74.9 us
    another operation x3, other arithmetic, shards(): jax.scipy.linalg.solve_triangular(factor, panel_rows.T, lower=True)  39.4 us
    psum x1, blocking collectives, shards(): col_mean = lax.psum(jnp.sum(widened, axis=0), 'smp') / sample_total  36.5 us
  transfers between devices with their start and end apart: 4, of which 4 were waited for; matrix products, arithmetic and copies ran while one was open for 0% of the time, Pallas kernels for 0%

commit v1 on v0

--- a/solution.py
+++ b/solution.py
@@ -1,3 +1,4 @@
+import functools
 import jax
 import jax.numpy as jnp
 from jax import lax
@@ -5,6 +6,25 @@
 
 PANEL = 512
 shift_scale = 0.01
+
+
+def scan_the_teams(field_in, comm_axis):
+    k_all = lax.axis_size(comm_axis)
+    series = tuple(((num, (num + 1) % k_all) for num in range(k_all)))
+    shelf = tuple(((num, (num - 1) % k_all) for num in range(k_all)))
+    block_now, inter = ([field_in], [field_in])
+    for _ in range(k_all // 2):
+        block_now.append(lax.ppermute(block_now[-1], comm_axis, series))
+    for _ in range((k_all - 1) // 2):
+        inter.append(lax.ppermute(inter[-1], comm_axis, shelf))
+    return jnp.roll(
+        jnp.concatenate([*block_now[::-1], *inter[1:]], axis=0),
+        (lax.axis_index(comm_axis) - k_all // 2) * field_in.shape[0],
+        axis=0,
+    )
+
+
+_place_regions = functools.partial(scan_the_teams, comm_axis="smp")
 
 
 def shards(jacobian):
@@ -19,7 +39,7 @@
     widened = jacobian.astype(jnp.float32)
     col_mean = lax.psum(jnp.sum(widened, axis=0), "smp") / sample_total
     centered = (widened - col_mean).astype(jnp.bfloat16)
-    gathered = lax.all_gather(centered, "smp", axis=0, tiled=True)
+    gathered = _place_regions(centered)
     gram_tile = lax.psum_scatter(
         lax.dot_general(
             gathered, centered, (((1,), (1,)), ((), ())), preferred_element_type=jnp.float32

time: 758 us -> 778 us (1.026)
  starting transfers between devices: 0.34 us -> 51.9 us
  waiting for transfers between devices: 447 us -> 402 us
  local copies, waits for them, and re-layouts: 14.6 us -> 23.1 us
    all_gather x1 -> x0, waiting for transfers between devices: 74.9 us -> none  [shards(): gathered = lax.all_gather(centered, 'smp', axis=0, tiled=True)]
    ppermute x0 -> x15, starting transfers between devices: none -> 51.3 us  [the longest x7 36.1 us: scan_the_teams(): inter.append(lax.ppermute(inter[-1], comm_axis, shelf))]
    ppermute x0 -> x15, waiting for transfers between devices: none -> 30.5 us  [the longest x8 30.5 us: scan_the_teams(): block_now.append(lax.ppermute(block_now[-1], comm_axis, series))]
  transfers between devices with their start and end apart: 4 -> 18, of which waited for: 4 -> 11; matrix products, arithmetic and copies ran while one was open for 0% -> 1% of each run, Pallas kernels for 0% -> 0%
where the time goes in v1:
time: 778 us; the launch traced here: 773 us
  waiting for transfers between devices  402 us (52%)
  blocking collectives  138 us (18%)
  other arithmetic  129 us (17%)
  starting transfers between devices  51.9 us (7%)
  local copies, waits for them, and re-layouts  23.1 us (3%)
  between operations  18.1 us (2%)
  matrix products  10.9 us (1%)
    psum x1, waiting for transfers between devices, shards(): square, band_rows = lax.psum((top_square, top_band), 'smp')  140 us
    psum x1, waiting for transfers between devices, shards(): panel_rows = lax.psum(placed_rows, 'par')  130 us
    psum x1, blocking collectives, shards(): lax.psum(jnp.sum(jnp.where(diag_mask, gram_tile, 0.0)), ('smp', 'par'))  102 us
    reduce_scatter x1, waiting for transfers between devices, shards(): lax.psum_scatter(lax.dot_general(gathered, centered, (((1,), (1,)), ((),...  101 us
    another operation x14, other arithmetic, shards(): factor = jnp.linalg.cholesky(square)  80.2 us
    another operation x3, other arithmetic, shards(): jax.scipy.linalg.solve_triangular(factor, panel_rows.T, lower=True)  40.7 us
    psum x1, blocking collectives, shards(): col_mean = lax.psum(jnp.sum(widened, axis=0), 'smp') / sample_total  36.5 us
    ppermute x7, starting transfers between devices, scan_the_teams(): inter.append(lax.ppermute(inter[-1], comm_axis, shelf))  36.1 us
  transfers between devices with their start and end apart: 18, of which 11 were waited for; matrix products, arithmetic and copies ran while one was open for 1% of the time, Pallas kernels for 0%

profile of v1, /device:TPU:2, one launch (start us, length us, event | category | flops | bytes accessed | tf_op | source)
XLA Modules:
  0.0 773.2 jit_solution(2732795589432317324)
XLA Ops:
  8.3 36.5 %psum.35 = f32[512]{0:T(512)S(1)} all-reduce(f32[512]{0:T(512)S(1)} %convert_reduce_fusion), channel_id=1, replica_groups=mesh['smp'=16,'par'=32] {'smp'}, use_global_device_ids=true, to_apply=%region_1.0 | all-reduce | flops 512 | bytes 4096 | tf_op jit(solution)/shard_map/psum | solution.py:40
  45.8 1.9 collective-permute-start
  47.7 10.2 %collective-permute-done = bf16[256,512]{1,0:T(8,128)(2,1)S(1)} collective-permute-done((bf16[256,512]{1,0:T(8,128)(2,1)S(1)}, bf16[256,512]{1,0:T(8,128)(2,1)S(1)}, u32[]{:S(2)}, u32[]{:S(2)}) %collective-permute-start) | collective-permute-done | bytes 262176 | tf_op jit(solution)/shard_map/ppermute | solution.py:17
  59.8 5.1 collective-permute-start.8
  65.0 4.4 collective-permute-done.1
  71.3 5.1 collective-permute-start.9
  76.4 3.5 collective-permute-done.2
  81.8 5.1 collective-permute-start.10
  87.0 2.6 collective-permute-done.3
  91.5 5.1 collective-permute-start.11
  96.6 2.4 collective-permute-done.4
  101.0 5.1 collective-permute-start.12
  106.1 2.4 collective-permute-done.5
  108.5 1.9 collective-permute-start.6
  110.4 5.1 collective-permute-start.13
  115.6 2.5 collective-permute-done.6
  120.0 5.3 collective-permute-start.14
  125.3 2.5 collective-permute-done.7
  134.5 3.2 convolution_multiply_fusion
  137.8 100.7 %reduce-scatter.2.cloned.1.call-done = f32[128,256]{1,0:T(8,128)} async-done(((f32[4096,256]{1,0:T(8,128)}), f32[128,256]{1,0:T(8,128)}) %reduce-scatter.2.cloned.1.call-update) | async-done | bytes 131088 | tf_op jit(solution)/shard_map/reduce_scatter | solution.py:43
  240.2 101.8 %psum.36 = f32[]{:T(128)} all-reduce(f32[]{:T(128)} %fusion.30), channel_id=1, replica_groups=mesh['smp'=16,'par'=32] {'smp','par'}, use_global_device_ids=true, to_apply=%region_4.5 | all-reduce | flops 1 | bytes 8 | tf_op jit(solution)/shard_map/psum | solution.py:55
  345.1 130.1 %all-reduce.5.cloned.1.call-done = f32[256,512]{0,1:T(8,128)} async-done(((f32[256,512]{0,1:T(8,128)}), f32[256,512]{0,1:T(8,128)}) %all-reduce.5.cloned.1.call-update) | async-done | bytes 524304 | tf_op jit(solution)/shard_map/psum | solution.py:63
  478.0 140.2 %all-reduce.7.cloned.1.call-done = (f32[512,512]{0,1:T(8,128)}, f32[512,128]{0,1:T(8,128)}) async-done(((f32[512,512]{0,1:T(8,128)}, f32[512,128]{0,1:T(8,128)}), (f32[512,512]{0,1:T(8,128)}, f32[512,128]{0,1:T(8,128)})) %all-reduce.7.cloned.1.call-update) | async-done | bytes 1310736 | tf_op jit(solution)/shard_map/psum | solution.py:72
  621.3 11.7 %cholesky.103 = f32[128,128]{1,0:T(8,128)S(1)} custom-call(f32[128,128]{1,0:T(8,128)S(1)} %cholesky.263), custom_call_target="Cholesky" | custom-call | tf_op jit(solution)/shard_map/jit(cholesky)/cholesky | solution.py:73
  633.0 9.8 %custom-call.34 = f32[1,128,128]{1,2,0:T(8,128)S(1)} custom-call(f32[1,128,128]{2,1,0:T(8,128)S(1)} %get-tuple-element.35), custom_call_target="InvertDiagBlocksLowerTriangular" | custom-call | tf_op jit(solution)/shard_map/jit(cholesky)/cholesky | solution.py:73
  643.5 11.7 %cholesky.215 = f32[128,128]{1,0:T(8,128)S(1)} custom-call(f32[128,128]{1,0:T(8,128)S(1)} %cholesky.267), custom_call_target="Cholesky" | custom-call | tf_op jit(solution)/shard_map/jit(cholesky)/cholesky | solution.py:73
  656.3 10.8 %custom-call.35 = f32[1,128,128]{1,2,0:T(8,128)S(1)} custom-call(f32[1,128,128]{2,1,0:T(8,128)} %get-tuple-element.33), custom_call_target="InvertDiagBlocksLowerTriangular" | custom-call | tf_op jit(solution)/shard_map/jit(cholesky)/cholesky | solution.py:73
  668.1 11.7 %cholesky.236 = f32[128,128]{1,0:T(8,128)S(1)} custom-call(f32[128,128]{1,0:T(8,128)S(1)} %cholesky.272), custom_call_target="Cholesky" | custom-call | tf_op jit(solution)/shard_map/jit(cholesky)/cholesky | solution.py:73
  680.0 9.8 %custom-call.36 = f32[1,128,128]{1,2,0:T(8,128)S(1)} custom-call(f32[1,128,128]{2,1,0:T(8,128)S(1)} %get-tuple-element.31), custom_call_target="InvertDiagBlocksLowerTriangular" | custom-call | tf_op jit(solution)/shard_map/jit(cholesky)/cholesky | solution.py:73
  690.6 11.9 %cholesky.253 = f32[128,128]{1,0:T(8,128)S(1)} custom-call(f32[128,128]{1,0:T(8,128)S(1)} %convolution_subtract_fusion.9), custom_call_target="Cholesky" | custom-call | tf_op jit(solution)/shard_map/jit(cholesky)/cholesky | solution.py:73
  707.9 11.2 %while.1 = (s32[]{:T(128)}, f32[512,512]{0,1:T(8,128)S(1)}, s32[4,2]{0,1:T(2,128)S(1)}, f32[4,128,128]{2,1,0:T(8,128)}, s32[]{:T(128)}) while((s32[]{:T(128)}, f32[512,512]{0,1:T(8,128)S(1)}, s32[4,2]{0,1:T(2,128)S(1)}, f32[4,128,128]{2,1,0:T(8,128)}, s32[]{:T(128)}) %tuple.30), condition=%wide.while_cond, body=%wide.while_body.sunk | while | flops 2 | bytes 393829 | solution.py:74
  719.1 40.1 %custom-call.37 = f32[4,128,128]{1,2,0:T(8,128)S(1)} custom-call(f32[4,128,128]{2,1,0:T(8,128)} %get-tuple-element.9), custom_call_target="InvertDiagBlocksLowerTriangular" | custom-call | tf_op jit(solution)/shard_map/jit(_solve_triangular)/triangular_solve | solution.py:74
  (150 shorter events, 54.6 us)
Async XLA Ops:
  7.2 127.1 %copy-start.1 = (bf16[256,512]{1,0:T(8,128)(2,1)S(1)}, bf16[256,512]{1,0:T(8,128)(2,1)}, u32[]{:S(2)}) copy-start(bf16[256,512]{1,0:T(8,128)(2,1)} %param.1) | copy-start | bytes 786436
  7.2 231.4 %reduce-scatter.2.cloned.1.call-start = ((), (), s32[]{:S(2)}) async-start(), calls=%async_computation.1 | async-start | bytes 4325376 | tf_op jit(solution)/shard_map/reduce_scatter | solution.py:43
  45.8 12.1 %collective-permute-start = (bf16[256,512]{1,0:T(8,128)(2,1)S(1)}, bf16[256,512]{1,0:T(8,128)(2,1)S(1)}, u32[]{:S(2)}, u32[]{:S(2)}) collective-permute-start(bf16[256,512]{1,0:T(8,128)(2,1)S(1)} %fusion.2), channel_id=1, source_target_pairs={{0,32},{32,64},{64,96},{96,128},{128,160},{160,192},{192,224},{224... | collective-permute-start | bytes 786440 | tf_op jit(solution)/shard_map/ppermute | solution.py:17
  57.9 11.4 %collective-permute-start.1 = (bf16[256,512]{1,0:T(8,128)(2,1)S(1)}, bf16[256,512]{1,0:T(8,128)(2,1)S(1)}, u32[]{:S(2)}, u32[]{:S(2)}) collective-permute-start(bf16[256,512]{1,0:T(8,128)(2,1)S(1)} %collective-permute-done), channel_id=1, source_target_pairs={{0,32},{32,64},{64,96},{96,128},{128,160},{160,192},{192,224},{224... | collective-permute-start | bytes 786440 | tf_op jit(solution)/shard_map/ppermute | solution.py:17
  59.8 11.4 %collective-permute-start.8 = (bf16[256,512]{1,0:T(8,128)(2,1)S(1)}, bf16[256,512]{1,0:T(8,128)(2,1)S(1)}, u32[]{:S(2)}, u32[]{:S(2)}) collective-permute-start(bf16[256,512]{1,0:T(8,128)(2,1)S(1)} %fusion.2), channel_id=1, source_target_pairs={{0,480},{32,0},{64,32},{96,64},{128,96},{160,128},{192,160},{224,1... | collective-permute-start | bytes 786440 | tf_op jit(solution)/shard_map/ppermute | solution.py:19
  69.3 10.6 %collective-permute-start.2 = (bf16[256,512]{1,0:T(8,128)(2,1)S(1)}, bf16[256,512]{1,0:T(8,128)(2,1)S(1)}, u32[]{:S(2)}, u32[]{:S(2)}) collective-permute-start(bf16[256,512]{1,0:T(8,128)(2,1)S(1)} %collective-permute-done.1), channel_id=1, source_target_pairs={{0,32},{32,64},{64,96},{96,128},{128,160},{160,192},{192,224},{224... | collective-permute-start | bytes 786440 | tf_op jit(solution)/shard_map/ppermute | solution.py:17
  71.3 10.6 %collective-permute-start.9 = (bf16[256,512]{1,0:T(8,128)(2,1)S(1)}, bf16[256,512]{1,0:T(8,128)(2,1)S(1)}, u32[]{:S(2)}, u32[]{:S(2)}) collective-permute-start(bf16[256,512]{1,0:T(8,128)(2,1)S(1)} %collective-permute-done.8), channel_id=1, source_target_pairs={{0,480},{32,0},{64,32},{96,64},{128,96},{160,128},{192,160},{224,1... | collective-permute-start | bytes 786440 | tf_op jit(solution)/shard_map/ppermute | solution.py:19
  79.9 9.7 %collective-permute-start.3 = (bf16[256,512]{1,0:T(8,128)(2,1)S(1)}, bf16[256,512]{1,0:T(8,128)(2,1)S(1)}, u32[]{:S(2)}, u32[]{:S(2)}) collective-permute-start(bf16[256,512]{1,0:T(8,128)(2,1)S(1)} %collective-permute-done.2), channel_id=1, source_target_pairs={{0,32},{32,64},{64,96},{96,128},{128,160},{160,192},{192,224},{224... | collective-permute-start | bytes 786440 | tf_op jit(solution)/shard_map/ppermute | solution.py:17
  81.8 9.7 %collective-permute-start.10 = (bf16[256,512]{1,0:T(8,128)(2,1)S(1)}, bf16[256,512]{1,0:T(8,128)(2,1)S(1)}, u32[]{:S(2)}, u32[]{:S(2)}) collective-permute-start(bf16[256,512]{1,0:T(8,128)(2,1)S(1)} %collective-permute-done.9), channel_id=1, source_target_pairs={{0,480},{32,0},{64,32},{96,64},{128,96},{160,128},{192,160},{224,1... | collective-permute-start | bytes 786440 | tf_op jit(solution)/shard_map/ppermute | solution.py:19
  89.6 9.5 %collective-permute-start.4 = (bf16[256,512]{1,0:T(8,128)(2,1)S(1)}, bf16[256,512]{1,0:T(8,128)(2,1)S(1)}, u32[]{:S(2)}, u32[]{:S(2)}) collective-permute-start(bf16[256,512]{1,0:T(8,128)(2,1)S(1)} %collective-permute-done.3), channel_id=1, source_target_pairs={{0,32},{32,64},{64,96},{96,128},{128,160},{160,192},{192,224},{224... | collective-permute-start | bytes 786440 | tf_op jit(solution)/shard_map/ppermute | solution.py:17
  91.5 9.5 %collective-permute-start.11 = (bf16[256,512]{1,0:T(8,128)(2,1)S(1)}, bf16[256,512]{1,0:T(8,128)(2,1)S(1)}, u32[]{:S(2)}, u32[]{:S(2)}) collective-permute-start(bf16[256,512]{1,0:T(8,128)(2,1)S(1)} %collective-permute-done.10), channel_id=1, source_target_pairs={{0,480},{32,0},{64,32},{96,64},{128,96},{160,128},{192,160},{224,1... | collective-permute-start | bytes 786440 | tf_op jit(solution)/shard_map/ppermute | solution.py:19
  99.0 9.5 %collective-permute-start.5 = (bf16[256,512]{1,0:T(8,128)(2,1)S(1)}, bf16[256,512]{1,0:T(8,128)(2,1)S(1)}, u32[]{:S(2)}, u32[]{:S(2)}) collective-permute-start(bf16[256,512]{1,0:T(8,128)(2,1)S(1)} %collective-permute-done.4), channel_id=1, source_target_pairs={{0,32},{32,64},{64,96},{96,128},{128,160},{160,192},{192,224},{224... | collective-permute-start | bytes 786440 | tf_op jit(solution)/shard_map/ppermute | solution.py:17
  101.0 9.5 %collective-permute-start.12 = (bf16[256,512]{1,0:T(8,128)(2,1)S(1)}, bf16[256,512]{1,0:T(8,128)(2,1)S(1)}, u32[]{:S(2)}, u32[]{:S(2)}) collective-permute-start(bf16[256,512]{1,0:T(8,128)(2,1)S(1)} %collective-permute-done.11), channel_id=1, source_target_pairs={{0,480},{32,0},{64,32},{96,64},{128,96},{160,128},{192,160},{224,1... | collective-permute-start | bytes 786440 | tf_op jit(solution)/shard_map/ppermute | solution.py:19
  108.5 1.9 copy-start.5
  108.5 9.6 %collective-permute-start.6 = (bf16[256,512]{1,0:T(8,128)(2,1)S(1)}, bf16[256,512]{1,0:T(8,128)(2,1)}, u32[]{:S(2)}, u32[]{:S(2)}) collective-permute-start(bf16[256,512]{1,0:T(8,128)(2,1)S(1)} %collective-permute-done.5), channel_id=1, source_target_pairs={{0,32},{32,64},{64,96},{96,128},{128,160},{160,192},{192,224},{224... | collective-permute-start | bytes 786440 | tf_op jit(solution)/shard_map/ppermute | solution.py:17
  110.4 9.6 %collective-permute-start.13 = (bf16[256,512]{1,0:T(8,128)(2,1)S(1)}, bf16[256,512]{1,0:T(8,128)(2,1)S(1)}, u32[]{:S(2)}, u32[]{:S(2)}) collective-permute-start(bf16[256,512]{1,0:T(8,128)(2,1)S(1)} %collective-permute-done.12), channel_id=1, source_target_pairs={{0,480},{32,0},{64,32},{96,64},{128,96},{160,128},{192,160},{224,1... | collective-permute-start | bytes 786440 | tf_op jit(solution)/shard_map/ppermute | solution.py:19
  118.1 9.8 %collective-permute-start.7 = (bf16[256,512]{1,0:T(8,128)(2,1)}, bf16[256,512]{1,0:T(8,128)(2,1)}, u32[]{:S(2)}, u32[]{:S(2)}) collective-permute-start(bf16[256,512]{1,0:T(8,128)(2,1)} %collective-permute-done.6), channel_id=1, source_target_pairs={{0,32},{32,64},{64,96},{96,128},{128,160},{160,192},{192,224},{224... | collective-permute-start | bytes 786440 | tf_op jit(solution)/shard_map/ppermute | solution.py:17
  120.0 14.0 %copy-start.6 = (bf16[256,512]{1,0:T(8,128)(2,1)S(1)}, bf16[256,512]{1,0:T(8,128)(2,1)}, u32[]{:S(2)}) copy-start(bf16[256,512]{1,0:T(8,128)(2,1)} %copy-done.5) | copy-start | bytes 786436
  120.0 12.0 %collective-permute-start.14 = (bf16[256,512]{1,0:T(8,128)(2,1)S(1)}, bf16[256,512]{1,0:T(8,128)(2,1)S(1)}, u32[]{:S(2)}, u32[]{:S(2)}) collective-permute-start(bf16[256,512]{1,0:T(8,128)(2,1)S(1)} %collective-permute-done.13), channel_id=1, source_target_pairs={{0,480},{32,0},{64,32},{96,64},{128,96},{160,128},{192,160},{224,1... | collective-permute-start | bytes 786440 | tf_op jit(solution)/shard_map/ppermute | solution.py:19
  137.7 337.4 %all-reduce.5.cloned.1.call-start = ((), (), s32[]{:S(2)}) async-start(), calls=%async_computation.2 | async-start | bytes 1048576 | tf_op jit(solution)/shard_map/psum | solution.py:63
  343.7 0.8 copy-start.3
  343.8 132.7 %copy-start.4 = (f32[512,128]{0,1:T(8,128)}, f32[512,128]{0,1:T(8,128)S(1)}, u32[]{:S(2)}) copy-start(f32[512,128]{0,1:T(8,128)S(1)} %get-tuple-element.28) | copy-start | bytes 786436
  344.6 273.6 %all-reduce.7.cloned.1.call-start = ((), (), s32[]{:S(2)}) async-start(), calls=%async_computation.3 | async-start | bytes 2621440 | tf_op jit(solution)/shard_map/psum | solution.py:72
  476.4 1.0 copy-start
  618.2 141.1 %copy-start.8 = (f32[512,128]{0,1:T(8,128)S(1)}, f32[512,128]{0,1:T(8,128)}, u32[]{:S(2)}) copy-start(f32[512,128]{0,1:T(8,128)} %get-tuple-element.25) | copy-start | bytes 786436
  618.2 143.4 %copy-start.2 = (f32[256,512]{0,1:T(8,128)S(1)}, f32[256,512]{0,1:T(8,128)}, u32[]{:S(2)}) copy-start(f32[256,512]{0,1:T(8,128)} %all-reduce.5.cloned.1.call-done) | copy-start | bytes 1572868
  621.3 142.9 %copy-start.7 = (f32[128,256]{1,0:T(8,128)S(1)}, f32[128,256]{1,0:T(8,128)}, u32[]{:S(2)}) copy-start(f32[128,256]{1,0:T(8,128)} %reduce-scatter.2.cloned.1.call-done) | copy-start | bytes 393220
Sparse Core Ops, SparseCore 0:
  137.8 100.6 reduce-scatter.1
  344.7 130.4 all-reduce.4
  477.6 140.5 all-reduce.6
